TPU v7x, 512 devices: a whole 4x4x16 slice. The times are simulated.
512 devices in a mesh: seq: 64 (over z, x), tp: 8 (over y, core).
Axes of the slice: x: 4, y: 4, z: 16, core: 2. Of those that a mesh axis runs over, the one named last changes fastest.
Arguments:
- mamba_x: bfloat16 [4096, 8192], P('seq', 'tp'), may hold values from -6 to 6
- gate_z: bfloat16 [4096, 8192], P('seq', 'tp'), may hold values from -6 to 6
- b_in: bfloat16 [4096, 1024], P('seq', 'tp'), may hold values from -1.25 to 1.25
- c_in: bfloat16 [4096, 1024], P('seq', 'tp'), may hold values from -1.25 to 1.25
- dt_raw: float32 [128, 4096], P('tp', 'seq'), may hold values from -2 to 24576
- a_log: float32 [128], P('tp'), may hold values from -14 to -3
- skip_d: float32 [128], P('tp'), may hold values from 0.5 to 1.5
- norm_gain: float32 [8192], P('tp'), may hold values from 0.5 to 1.5
- value_weight: bfloat16 [8192, 1024], P('tp'), may hold values from -0.09375 to 0.09375
- queries: bfloat16 [4096, 4096], P('seq', 'tp'), may hold values from -18 to 18
- keys: bfloat16 [4096, 1024], P('seq', 'tp'), may hold values from -4.5 to 4.5
Outputs:
- mamba_out: bfloat16 [4096, 8192], P('seq', 'tp')
- attention: bfloat16 [4096, 4096], P('seq', 'tp')
All inputs are finite; a program needn't handle non-finite values.
Results may differ from a plain program's by a relative error of at most 0.02.
Values may be sent and summed in bfloat16 or wider, within the bound.
No kernel may reach another device: no remote copies, remote signals or barrier semaphores. Data moves between devices by JAX's collectives and lax.ppermute only.
A program may use at most 128 MiB of HBM per device.

v0:
```python
import math
import jax
import jax.numpy as jnp
from jax import lax
from jax.sharding import PartitionSpec as P

MHEAD_DIM = 64
STATE = 128
QHEADS = 32
KVHEADS = 8
HEAD_DIM = 128
highest = lax.Precision.HIGHEST
norm_eps = 1e-05


def carried_in(part, axis, combine, identity):
    place = lax.axis_index(axis)
    gathered = jax.tree.map(lambda a: lax.all_gather(a, axis), part)
    state = jax.tree.map(lambda a, e: jnp.zeros_like(a) + jnp.asarray(e, a.dtype), part, identity)

    def one(lap, state):
        return combine(
            state, jax.tree.map(lambda a: lax.dynamic_index_in_dim(a, lap, 0, False), gathered)
        )

    return lax.fori_loop(0, place, one, state)


def block_scan(inputs, b_group, c_group, time_step, decay_rate):
    token_count = inputs.shape[0]
    log_decay = jnp.cumsum(-time_step * decay_rate[..., None], axis=2)
    log_gaps = log_decay[..., :, None] - log_decay[..., None, :]
    causal = jnp.arange(token_count)[:, None] >= jnp.arange(token_count)[None, :]
    decay_mat = jnp.exp(jnp.where(causal, log_gaps, -jnp.inf))
    cross_terms = jnp.einsum("tgn,sgn->gts", c_group, b_group, precision=highest)
    mixing = cross_terms[:, None] * decay_mat * time_step[:, :, None, :]
    local_out = jnp.einsum("gkts,sgkp->tgkp", mixing, inputs, precision=highest)
    tail_weight = jnp.exp(log_decay[..., -1:] - log_decay) * time_step
    summary = jnp.einsum("gks,sgkp,sgn->gkpn", tail_weight, inputs, b_group, precision=highest)
    return (log_decay, local_out, summary, jnp.exp(log_decay[..., -1]))


def carried_out(c_group, state_in, log_decay):
    carried_term = jnp.einsum("tgn,gkpn->tgkp", c_group, state_in, precision=highest)
    return carried_term * jnp.transpose(jnp.exp(log_decay), (2, 0, 1))[..., None]


def gated_norm(ssm_out, gate_z, norm_gain, group_count):
    token_count = ssm_out.shape[0]
    gated = ssm_out * jax.nn.silu(gate_z.astype(jnp.float32))
    grouped = gated.reshape(token_count, group_count, -1)
    inverse = lax.rsqrt(jnp.mean(grouped * grouped, axis=2, keepdims=True) + norm_eps)
    return ((grouped * inverse).reshape(token_count, -1) * norm_gain).astype(jnp.bfloat16)


def chain_combine(earlier, latter):
    return (earlier[0] * latter[0], latter[0][..., None, None] * earlier[1] + latter[1])


def query_layout(payload, kv_here, per_kv):
    count_rows = payload.shape[0]
    shaped = payload.reshape(count_rows, kv_here, per_kv, HEAD_DIM)
    return jnp.transpose(shaped, (1, 2, 0, 3)).reshape(kv_here, per_kv * count_rows, HEAD_DIM)


def row_positions(first_pos, count_rows, per_kv):
    return jnp.tile(first_pos + jnp.arange(count_rows, dtype=jnp.int32), per_kv)


def set_output(finished_set, kv_here, per_kv):
    running_max, running_sum, running_out = finished_set
    count_rows = running_sum.shape[1] // per_kv
    result = (running_out / running_sum[..., None]).astype(jnp.bfloat16)
    result = result.reshape(kv_here, per_kv, count_rows, HEAD_DIM)
    return jnp.transpose(result, (2, 0, 1, 3)).reshape(count_rows, kv_here * per_kv * HEAD_DIM)


def attend(running, query_set, key_slab, value_slab, key_first):
    query_block, query_pos = query_set
    score_scale = 1.0 / math.sqrt(HEAD_DIM)
    key_pos = key_first + jnp.arange(key_slab.shape[1], dtype=jnp.int32)

    def update(current):
        running_max, running_sum, running_out = current
        scores = (
            jnp.einsum("hrd,hcd->hrc", query_block, key_slab, preferred_element_type=jnp.float32)
            * score_scale
        )
        allowed = key_pos[None, :] <= query_pos[:, None]
        scores = jnp.where(allowed[None], scores, -jnp.inf)
        new_max = jnp.maximum(running_max, jnp.max(scores, axis=2))
        weights = jnp.exp(scores - new_max[..., None])
        shrink = jnp.exp(running_max - new_max)
        new_sum = running_sum * shrink + jnp.sum(weights, axis=2)
        new_out = running_out * shrink[..., None] + jnp.einsum(
            "hrc,hcd->hrd",
            weights.astype(jnp.bfloat16),
            value_slab,
            preferred_element_type=jnp.float32,
        )
        return (new_max, new_sum, new_out)

    def unchanged(current):
        return current

    return lax.cond(key_first <= jnp.max(query_pos), update, unchanged, running)


def per_device(
    mamba_x, gate_z, b_in, c_in, dt_raw, a_log, skip_d, norm_gain, value_weight, queries, keys
):
    tokens_here = mamba_x.shape[0]
    group_count = b_in.shape[1] // STATE
    head_count = dt_raw.shape[0]
    per_group = head_count // group_count
    inputs = mamba_x.astype(jnp.float32).reshape(tokens_here, group_count, per_group, MHEAD_DIM)
    b_group = b_in.astype(jnp.float32).reshape(tokens_here, group_count, STATE)
    c_group = c_in.astype(jnp.float32).reshape(tokens_here, group_count, STATE)
    time_step = jax.nn.softplus(dt_raw).reshape(group_count, per_group, tokens_here)
    decay_rate = jnp.exp(a_log).reshape(group_count, per_group)
    log_decay, local_out, summary, totals = block_scan(
        inputs, b_group, c_group, time_step, decay_rate
    )
    _, state_in = carried_in(
        (totals, summary), "seq", chain_combine, (jnp.ones_like(totals), jnp.zeros_like(summary))
    )
    skip_heads = skip_d.reshape(group_count, per_group)[None, :, :, None]
    ssm_out = local_out + carried_out(c_group, state_in, log_decay) + skip_heads * inputs
    mamba_out = gated_norm(ssm_out.reshape(tokens_here, -1), gate_z, norm_gain, group_count)
    kv_here = keys.shape[1] // HEAD_DIM
    per_kv = QHEADS // KVHEADS
    product = jnp.dot(mamba_out, value_weight, preferred_element_type=jnp.float32)
    values = lax.psum_scatter(
        jnp.transpose(
            product.reshape(tokens_here, lax.axis_size("tp") * kv_here, HEAD_DIM), (1, 0, 2)
        ).astype(jnp.bfloat16),
        "tp",
        scatter_dimension=0,
        tiled=True,
    )
    key_heads = jnp.transpose(keys.reshape(tokens_here, kv_here, HEAD_DIM), (1, 0, 2))
    my_index = lax.axis_index("seq")
    query_sets = [
        (
            query_layout(queries, kv_here, per_kv),
            row_positions(my_index * tokens_here, tokens_here, per_kv),
        )
    ]
    initial = tuple(
        (
            (
                jnp.full((kv_here, query_set[0].shape[1]), -jnp.inf, jnp.float32),
                jnp.zeros((kv_here, query_set[0].shape[1]), jnp.float32),
                jnp.zeros((kv_here, query_set[0].shape[1], HEAD_DIM), jnp.float32),
            )
            for query_set in query_sets
        )
    )
    key_portion = lax.all_gather(key_heads, "seq", axis=1, tiled=True)
    value_portion = lax.all_gather(values, "seq", axis=1, tiled=True)
    length = key_portion.shape[1]
    block_len = length
    for multiple in (1, 2, 4):
        block_len = multiple * tokens_here

    def one_block(block_index, current):
        offset = block_index * block_len
        key_slab = lax.dynamic_slice_in_dim(key_portion, offset, block_len, 1)
        value_slab = lax.dynamic_slice_in_dim(value_portion, offset, block_len, 1)
        return tuple(
            (
                attend(current[set_index], query_sets[set_index], key_slab, value_slab, offset)
                for set_index in range(len(query_sets))
            )
        )

    finished = lax.fori_loop(0, length // block_len, one_block, initial)
    outputs = [set_output(finished_set, kv_here, per_kv) for finished_set in finished]
    attention = outputs[0]
    return (mamba_out, attention)


def solution(mesh):
    placed = (
        P("seq", "tp"),
        P("seq", "tp"),
        P("seq", "tp"),
        P("seq", "tp"),
        P("tp", "seq"),
        P("tp"),
        P("tp"),
        P("tp"),
        P("tp", None),
        P("seq", "tp"),
        P("seq", "tp"),
    )
    return jax.shard_map(
        per_device,
        mesh=mesh,
        in_specs=placed,
        out_specs=(P("seq", "tp"), P("seq", "tp")),
        check_vma=False,
    )
```

profile of v0, /device:TPU:480, one launch (start us, length us, event | category | flops | bytes accessed | tf_op | source)
XLA Modules:
  0.0 750.5 jit_solution(6143692668134072282)
XLA Ops:
  10.9 1.2 fusion.21
  13.3 2.9 copy.71
  16.2 72.4 %all-gather = f32[64,16,1]{1,2,0:T(1,128)S(1)} all-gather(f32[1,16,1]{1,2,0:T(1,128)S(1)} %exp.63), channel_id=2, replica_groups=mesh['seq'=64,'tp'=8] {'seq'}, dimensions={0}, use_global_device_ids=true | all-gather | bytes 4160 | tf_op jit(solution)/shard_map/all_gather | solution.py:18
  88.7 1.5 convolution_bitcast_fusion.2
  90.2 212.9 %all-gather.9.cloned.1.call-done = f32[1024,64,128]{2,1,0:T(8,128)} async-done(((f32[16,64,128]{2,1,0:T(8,128)}), f32[1024,64,128]{2,1,0:T(8,128)}) %all-gather.9.cloned.1.call-update) | async-done | bytes 33554448 | tf_op jit(solution)/shard_map/all_gather | solution.py:18
  303.2 74.1 %while.32 = (s32[]{:T(128)}, f32[1,16,64,128]{3,2,1,0:T(8,128)S(1)}, s32[]{:T(128)}, f32[64,1,16]{2,1,0:T(1,128)S(1)}, f32[64,1,16,64,128]{4,3,2,1,0:T(8,128)}, /*index=5*/s32[]{:T(128)}, s32[]{:T(128)}, s32[]{:T(128)}) while((s32[]{:T(128)}, f32[1,16,64,128]{3,2,1,0:T(8,128)S(1)}, s32[]{:T(128)}, f32[64,1,16]{2,1,0:T(1,128)S(1)}, ...), condition=%wide.region_2.3_spmd, body=%wide.region_1.2_spmd.sunk | while | flops 262149 | bytes 1573183 | solution.py:26
  303.2 1.2 bitcast_add_fusion.2
  304.5 1.2 bitcast_add_fusion.2
  305.7 1.2 bitcast_add_fusion.2
  306.9 1.2 bitcast_add_fusion.2
  308.2 1.2 bitcast_add_fusion.2
  309.4 1.2 bitcast_add_fusion.2
  310.6 1.2 bitcast_add_fusion.2
  311.9 1.2 bitcast_add_fusion.2
  313.1 1.2 bitcast_add_fusion.2
  314.3 1.2 bitcast_add_fusion.2
  315.6 1.2 bitcast_add_fusion.2
  316.8 1.2 bitcast_add_fusion.2
  318.0 1.2 bitcast_add_fusion.2
  319.3 1.2 bitcast_add_fusion.2
  320.5 1.2 bitcast_add_fusion.2
  321.7 1.2 bitcast_add_fusion.2
  323.0 1.2 bitcast_add_fusion.2
  324.2 1.2 bitcast_add_fusion.2
  325.4 1.2 bitcast_add_fusion.2
  326.7 1.2 bitcast_add_fusion.2
  332.9 1.2 bitcast_add_fusion.2
  334.1 1.2 bitcast_add_fusion.2
  340.3 1.2 bitcast_add_fusion.2
  341.5 1.2 bitcast_add_fusion.2
  342.7 1.2 bitcast_add_fusion.2
  347.7 1.2 bitcast_add_fusion.2
  348.9 1.2 bitcast_add_fusion.2
  350.1 1.2 bitcast_add_fusion.2
  356.3 1.2 bitcast_add_fusion.2
  357.5 1.2 bitcast_add_fusion.2
  363.7 1.2 bitcast_add_fusion.2
  365.0 1.2 bitcast_add_fusion.2
  366.2 1.2 bitcast_add_fusion.2
  371.1 1.2 bitcast_add_fusion.2
  372.4 1.2 bitcast_add_fusion.2
  373.6 1.2 bitcast_add_fusion.2
  377.3 2.0 fusion.18
  380.2 1.4 fusion.19
  382.4 33.4 %reduce-scatter.2.cloned.1.call-done = bf16[1,64,128]{2,1,0:T(8,128)(2,1)} async-done(((bf16[8,64,128]{2,1,0:T(8,128)(2,1)}), bf16[1,64,128]{2,1,0:T(8,128)(2,1)}) %reduce-scatter.2.cloned.1.call-update) | async-done | bytes 16400 | tf_op jit(solution)/shard_map/reduce_scatter | solution.py:133
  416.7 138.2 %all-gather.11.cloned.1.call-done = bf16[4096,128]{1,0:T(8,128)(2,1)} async-done(((bf16[64,128]{1,0:T(8,128)(2,1)}), bf16[4096,128]{1,0:T(8,128)(2,1)}) %all-gather.11.cloned.1.call-update) | async-done | bytes 1048592 | tf_op jit(solution)/shard_map/all_gather | solution.py:159
  554.8 138.3 %all-gather.7.cloned.1.call-done = bf16[1,4096,128]{2,1,0:T(8,128)(2,1)} async-done(((bf16[1,64,128]{2,1,0:T(8,128)(2,1)}), bf16[1,4096,128]{2,1,0:T(8,128)(2,1)}) %all-gather.7.cloned.1.call-update) | async-done | bytes 1048592 | tf_op jit(solution)/shard_map/all_gather | solution.py:160
  693.1 50.0 %while.33 = (s32[]{:T(128)}, f32[1,256]{1,0:T(1,128)S(1)}, f32[1,256]{1,0:T(1,128)S(1)}, f32[1,256,128]{2,1,0:T(8,128)S(1)}, s32[]{:T(128)}, /*index=5*/bf16[1,4...) while((s32[]{:T(128)}, f32[1,256]{1,0:T(1,128)S(1)}, ...), condition=%wide.region_11.12_spmd.clone, body=%wide.region_6.11_spmd.clone.sunk | while | flops 34145032 | bytes 1270325 | solution.py:177
  693.8 2.4 conditional.3
  697.0 2.4 conditional.3
  700.1 2.4 conditional.3
  703.2 2.4 conditional.3
  706.3 2.4 conditional.3
  709.5 2.4 conditional.3
  712.6 2.4 conditional.3
  715.7 2.4 conditional.3
  718.8 2.4 conditional.3
  721.9 2.4 conditional.3
  725.1 2.4 conditional.3
  728.2 2.4 conditional.3
  731.3 2.4 conditional.3
  734.4 2.4 conditional.3
  737.6 2.4 conditional.3
  740.7 2.4 conditional.3
  (294 shorter events, 74.8 us)
Async XLA Ops:
  7.2 3.7 copy-start
  7.2 295.9 %all-gather.9.cloned.1.call-start = ((), (), s32[]{:S(2)}) async-start(), calls=%async_computation.3 | async-start | bytes 34078720 | tf_op jit(solution)/shard_map/all_gather | solution.py:18
  12.2 403.7 %reduce-scatter.2.cloned.1.call-start = ((), (), s32[]{:S(2)}) async-start(), calls=%async_computation.1 | async-start | bytes 147456 | tf_op jit(solution)/shard_map/reduce_scatter | solution.py:133
  13.3 75.3 %copy-start.3 = (bf16[64,128]{1,0:T(8,128)(2,1)S(1)}, bf16[64,128]{1,0:T(8,128)(2,1)}, u32[]{:S(2)}) copy-start(bf16[64,128]{1,0:T(8,128)(2,1)} %param.20) | copy-start | bytes 49156
  303.2 74.1 %copy-start.6 = (f32[16]{0:T(128)S(1)}, f32[16]{0:T(128)}, u32[]{:S(2)}) copy-start(f32[16]{0:T(128)} %param.23) | copy-start | bytes 196
  377.3 2.6 copy-start.2
  377.3 2.8 copy-start.5
  379.7 36.2 %copy-start.4 = (bf16[64,512]{1,0:T(8,128)(2,1)S(1)}, bf16[64,512]{1,0:T(8,128)(2,1)}, u32[]{:S(2)}) copy-start(bf16[64,512]{1,0:T(8,128)(2,1)} %param.26) | copy-start | bytes 196612
  380.2 312.9 %copy-start.1 = (bf16[64,1024]{1,0:T(8,128)(2,1)}, bf16[64,1024]{1,0:T(8,128)(2,1)S(1)}, u32[]{:S(2)}) copy-start(bf16[64,1024]{1,0:T(8,128)(2,1)S(1)} %multiply_convert_fusion) | copy-start | bytes 393220
  381.6 173.2 %all-gather.11.cloned.1.call-start = ((), (), s32[]{:S(2)}) async-start(), calls=%async_computation.4 | async-start | bytes 1064960 | tf_op jit(solution)/shard_map/all_gather | solution.py:159
  382.4 310.7 %all-gather.7.cloned.1.call-start = ((), (), s32[]{:S(2)}) async-start(), calls=%async_computation.2 | async-start | bytes 1064960 | tf_op jit(solution)/shard_map/all_gather | solution.py:160
Sparse Core Ops, SparseCore 0:
  12.3 290.7 all-gather.8
  381.8 34.0 reduce-scatter.1
  419.2 135.5 all-gather.10
  558.0 134.9 all-gather.6
where the time goes:
time: 755 us; the launch traced here: 750 us
  waiting for transfers between devices  523 us (69%)
  other arithmetic  75.7 us (10%)
  blocking collectives  72.4 us (10%)
  matrix products  41 us (5%)
  loops' own time  14.7 us (2%)
  between operations  14 us (2%)
  local copies, waits for them, and re-layouts  9.01 us (1%)
    all_gather x1, waiting for transfers between devices, carried_in(): gathered = jax.tree.map(lambda a: lax.all_gather(a, axis), part)  213 us
    all_gather x1, waiting for transfers between devices, per_device(): value_portion = lax.all_gather(values, 'seq', axis=1, tiled=True)  138 us
    all_gather x1, waiting for transfers between devices, per_device(): key_portion = lax.all_gather(key_heads, 'seq', axis=1, tiled=True)  138 us
    all_gather x1, blocking collectives, carried_in(): gathered = jax.tree.map(lambda a: lax.all_gather(a, axis), part)  72.4 us
    add x60, other arithmetic, chain_combine(): latter[0][..., None, None] * earlier[1] + latter[1]  71.2 us
    reduce_scatter x1, waiting for transfers between devices, per_device(): lax.psum_scatter(jnp.transpose(product.reshape(tokens_here, lax.axis_size...  33.4 us
    dot_general x16, matrix products, update(): jnp.einsum('hrc,hcd->hrd', weights.astype(jnp.bfloat16), value_slab, pref...  17.8 us
    dot_general x16, matrix products, update(): jnp.einsum('hrd,hcd->hrc', query_block, key_slab, preferred_element_type=...  17 us
  transfers between devices with their start and end apart: 4, of which 4 were waited for; matrix products, arithmetic and copies ran while one was open for 1% of the time, Pallas kernels for 0%

commit v1 on v0

--- a/solution.py
+++ b/solution.py
@@ -156,7 +156,10 @@
             for query_set in query_sets
         )
     )
-    key_portion = lax.all_gather(key_heads, "seq", axis=1, tiled=True)
+    size = lax.axis_size("seq")
+    blocks = jnp.stack([key_heads for _ in range(size)])
+    blocks = lax.all_to_all(blocks, "seq", split_axis=0, concat_axis=0)
+    key_portion = jnp.concatenate(blocks, axis=1)
     value_portion = lax.all_gather(values, "seq", axis=1, tiled=True)
     length = key_portion.shape[1]
     block_len = length

time: 755 us -> 655 us (0.87)
  waiting for transfers between devices: 523 us -> 363 us
  blocking collectives: 72.4 us -> 121 us
  starting transfers between devices: 0.16 us -> 12.5 us
    all_gather x1 -> x0, waiting for transfers between devices: 138 us -> none  [per_device(): key_portion = lax.all_gather(key_heads, 'seq', axis=1, tiled=True)]
    all_gather x1, blocking collectives: 72.4 us -> 121 us  [carried_in(): gathered = jax.tree.map(lambda a: lax.all_gather(a, axis), part)]
    all_gather x1, waiting for transfers between devices: 213 us -> 190 us  [carried_in(): gathered = jax.tree.map(lambda a: lax.all_gather(a, axis), part)]
    all_to_all x0 -> x1, starting transfers between devices: none -> 12.3 us  [per_device(): blocks = lax.all_to_all(blocks, 'seq', split_axis=0, concat_axis=0)]
  transfers between devices with their start and end apart: 4 -> 4, of which waited for: 4 -> 3; matrix products, arithmetic and copies ran while one was open for 1% -> 13% of each run, Pallas kernels for 0% -> 0%
where the time goes in v1:
time: 655 us; the launch traced here: 650 us
  waiting for transfers between devices  363 us (55%)
  blocking collectives  121 us (18%)
  other arithmetic  75.6 us (12%)
  matrix products  40.9 us (6%)
  loops' own time  14.1 us (2%)
  between operations  14 us (2%)
  starting transfers between devices  12.5 us (2%)
  local copies, waits for them, and re-layouts  10.1 us (2%)
    all_gather x1, waiting for transfers between devices, carried_in(): gathered = jax.tree.map(lambda a: lax.all_gather(a, axis), part)  190 us
    all_gather x1, waiting for transfers between devices, per_device(): value_portion = lax.all_gather(values, 'seq', axis=1, tiled=True)  138 us
    all_gather x1, blocking collectives, carried_in(): gathered = jax.tree.map(lambda a: lax.all_gather(a, axis), part)  121 us
    add x60, other arithmetic, chain_combine(): latter[0][..., None, None] * earlier[1] + latter[1]  71.2 us
    reduce_scatter x1, waiting for transfers between devices, per_device(): lax.psum_scatter(jnp.transpose(product.reshape(tokens_here, lax.axis_size...  34.2 us
    dot_general x16, matrix products, update(): jnp.einsum('hrc,hcd->hrd', weights.astype(jnp.bfloat16), value_slab, pref...  17.8 us
    dot_general x16, matrix products, update(): jnp.einsum('hrd,hcd->hrc', query_block, key_slab, preferred_element_type=...  16.9 us
  transfers between devices with their start and end apart: 4, of which 3 were waited for; matrix products, arithmetic and copies ran while one was open for 13% of the time, Pallas kernels for 0%

profile of v1, /device:TPU:480, one launch (start us, length us, event | category | flops | bytes accessed | tf_op | source)
XLA Modules:
  0.0 650.4 jit_solution(16742029486299079433)
XLA Ops:
  10.9 1.2 fusion.21
  12.1 2.0 stack.3
  14.1 12.3 %all-to-all-start = ((bf16[64,1,64,128]{3,2,1,0:T(8,128)(2,1)}), bf16[64,1,64,128]{3,2,1,0:T(8,128)(2,1)}, u32[]{:S(2)}, u32[]{:S(2)}) async-start(bf16[64,1,64,128]{3,2,1,0:T(8,128)(2,1)} %stack.3), calls=%async_computation | async-start | bytes 2097152 | tf_op jit(solution)/shard_map/all_to_all | solution.py:161
  26.7 2.9 copy.71
  29.6 120.6 %all-gather = f32[64,16,1]{1,2,0:T(1,128)S(1)} all-gather(f32[1,16,1]{1,2,0:T(1,128)S(1)} %exp.63), channel_id=2, replica_groups=mesh['seq'=64,'tp'=8] {'seq'}, dimensions={0}, use_global_device_ids=true | all-gather | bytes 4160 | tf_op jit(solution)/shard_map/all_gather | solution.py:18
  150.3 1.5 convolution_bitcast_fusion.2
  151.8 190.2 %all-gather.7.cloned.1.call-done = f32[1024,64,128]{2,1,0:T(8,128)} async-done(((f32[16,64,128]{2,1,0:T(8,128)}), f32[1024,64,128]{2,1,0:T(8,128)}) %all-gather.7.cloned.1.call-update) | async-done | bytes 33554448 | tf_op jit(solution)/shard_map/all_gather | solution.py:18
  342.1 74.1 %while.32 = (s32[]{:T(128)}, f32[1,16,64,128]{3,2,1,0:T(8,128)S(1)}, s32[]{:T(128)}, f32[64,1,16]{2,1,0:T(1,128)S(1)}, f32[64,1,16,64,128]{4,3,2,1,0:T(8,128)}, /*index=5*/s32[]{:T(128)}, s32[]{:T(128)}, s32[]{:T(128)}) while((s32[]{:T(128)}, f32[1,16,64,128]{3,2,1,0:T(8,128)S(1)}, s32[]{:T(128)}, f32[64,1,16]{2,1,0:T(1,128)S(1)}, ...), condition=%wide.region_2.3_spmd, body=%wide.region_1.2_spmd.sunk | while | flops 262149 | bytes 1573183 | solution.py:26
  342.1 1.2 bitcast_add_fusion.2
  343.3 1.2 bitcast_add_fusion.2
  344.6 1.2 bitcast_add_fusion.2
  345.8 1.2 bitcast_add_fusion.2
  347.0 1.2 bitcast_add_fusion.2
  348.3 1.2 bitcast_add_fusion.2
  349.5 1.2 bitcast_add_fusion.2
  350.7 1.2 bitcast_add_fusion.2
  352.0 1.2 bitcast_add_fusion.2
  353.2 1.2 bitcast_add_fusion.2
  354.4 1.2 bitcast_add_fusion.2
  355.7 1.2 bitcast_add_fusion.2
  356.9 1.2 bitcast_add_fusion.2
  358.1 1.2 bitcast_add_fusion.2
  359.4 1.2 bitcast_add_fusion.2
  360.6 1.2 bitcast_add_fusion.2
  361.8 1.2 bitcast_add_fusion.2
  363.1 1.2 bitcast_add_fusion.2
  368.0 1.2 bitcast_add_fusion.2
  369.3 1.2 bitcast_add_fusion.2
  370.5 1.2 bitcast_add_fusion.2
  376.7 1.2 bitcast_add_fusion.2
  377.9 1.2 bitcast_add_fusion.2
  384.1 1.2 bitcast_add_fusion.2
  385.3 1.2 bitcast_add_fusion.2
  386.5 1.2 bitcast_add_fusion.2
  391.5 1.2 bitcast_add_fusion.2
  392.7 1.2 bitcast_add_fusion.2
  393.9 1.2 bitcast_add_fusion.2
  400.1 1.2 bitcast_add_fusion.2
  401.4 1.2 bitcast_add_fusion.2
  407.5 1.2 bitcast_add_fusion.2
  408.8 1.2 bitcast_add_fusion.2
  410.0 1.2 bitcast_add_fusion.2
  414.9 1.2 bitcast_add_fusion.2
  416.2 2.0 fusion.18
  419.1 1.4 fusion.19
  420.5 34.2 %reduce-scatter.2.cloned.1.call-done = bf16[1,64,128]{2,1,0:T(8,128)(2,1)} async-done(((bf16[8,64,128]{2,1,0:T(8,128)(2,1)}), bf16[1,64,128]{2,1,0:T(8,128)(2,1)}) %reduce-scatter.2.cloned.1.call-update) | async-done | bytes 16400 | tf_op jit(solution)/shard_map/reduce_scatter | solution.py:133
  455.5 138.2 %all-gather.5.cloned.1.call-done = bf16[1,4096,128]{2,1,0:T(8,128)(2,1)} async-done(((bf16[1,64,128]{2,1,0:T(8,128)(2,1)}), bf16[1,4096,128]{2,1,0:T(8,128)(2,1)}) %all-gather.5.cloned.1.call-update) | async-done | bytes 1048592 | tf_op jit(solution)/shard_map/all_gather | solution.py:163
  593.7 49.3 %while.33 = (s32[]{:T(128)}, f32[1,256]{1,0:T(1,128)S(1)}, f32[1,256]{1,0:T(1,128)S(1)}, f32[1,256,128]{2,1,0:T(8,128)S(1)}, s32[]{:T(128)}, /*index=5*/bf16[1,4...) while((s32[]{:T(128)}, f32[1,256]{1,0:T(1,128)S(1)}, ...), condition=%wide.region_11.12_spmd.clone, body=%wide.region_6.11_spmd.clone.sunk | while | flops 34145032 | bytes 1270325 | solution.py:180
  594.4 2.4 conditional.3
  597.5 2.4 conditional.3
  600.6 2.4 conditional.3
  603.6 2.4 conditional.3
  606.7 2.4 conditional.3
  609.8 2.4 conditional.3
  612.9 2.4 conditional.3
  616.0 2.4 conditional.3
  619.0 2.4 conditional.3
  622.1 2.4 conditional.3
  625.2 2.4 conditional.3
  628.3 2.4 conditional.3
  631.4 2.4 conditional.3
  634.5 2.4 conditional.3
  637.5 2.4 conditional.3
  640.6 2.4 conditional.3
  (296 shorter events, 74.3 us)
Async XLA Ops:
  7.2 3.7 copy-start
  7.2 334.8 %all-gather.7.cloned.1.call-start = ((), (), s32[]{:S(2)}) async-start(), calls=%async_computation.4 | async-start | bytes 34078720 | tf_op jit(solution)/shard_map/all_gather | solution.py:18
  10.9 15.6 %copy-start.1 = (bf16[64,1024]{1,0:T(8,128)(2,1)S(1)}, bf16[64,1024]{1,0:T(8,128)(2,1)}, u32[]{:S(2)}) copy-start(bf16[64,1024]{1,0:T(8,128)(2,1)} %param.17) | copy-start | bytes 393220
  14.1 441.3 %all-to-all-start = ((bf16[64,1,64,128]{3,2,1,0:T(8,128)(2,1)}), bf16[64,1,64,128]{3,2,1,0:T(8,128)(2,1)}, u32[]{:S(2)}, u32[]{:S(2)}) async-start(bf16[64,1,64,128]{3,2,1,0:T(8,128)(2,1)} %stack.3), calls=%async_computation | async-start | bytes 2097152 | tf_op jit(solution)/shard_map/all_to_all | solution.py:161
  26.5 428.2 %reduce-scatter.2.cloned.1.call-start = ((), (), s32[]{:S(2)}) async-start(), calls=%async_computation.2 | async-start | bytes 147456 | tf_op jit(solution)/shard_map/reduce_scatter | solution.py:133
  26.7 123.5 %copy-start.4 = (bf16[64,128]{1,0:T(8,128)(2,1)S(1)}, bf16[64,128]{1,0:T(8,128)(2,1)}, u32[]{:S(2)}) copy-start(bf16[64,128]{1,0:T(8,128)(2,1)} %param.20) | copy-start | bytes 49156
  342.0 74.1 %copy-start.7 = (f32[16]{0:T(128)S(1)}, f32[16]{0:T(128)}, u32[]{:S(2)}) copy-start(f32[16]{0:T(128)} %param.23) | copy-start | bytes 196
  416.1 2.6 copy-start.3
  416.2 2.8 copy-start.6
  418.5 36.2 %copy-start.5 = (bf16[64,512]{1,0:T(8,128)(2,1)S(1)}, bf16[64,512]{1,0:T(8,128)(2,1)}, u32[]{:S(2)}) copy-start(bf16[64,512]{1,0:T(8,128)(2,1)} %param.26) | copy-start | bytes 196612
  419.1 174.7 %copy-start.2 = (bf16[64,1024]{1,0:T(8,128)(2,1)}, bf16[64,1024]{1,0:T(8,128)(2,1)S(1)}, u32[]{:S(2)}) copy-start(bf16[64,1024]{1,0:T(8,128)(2,1)S(1)} %multiply_convert_fusion) | copy-start | bytes 393220
  420.5 173.2 %all-gather.5.cloned.1.call-start = ((), (), s32[]{:S(2)}) async-start(), calls=%async_computation.3 | async-start | bytes 1064960 | tf_op jit(solution)/shard_map/all_gather | solution.py:163
Sparse Core Ops, SparseCore 0:
  12.3 329.6 all-gather.6
  420.6 34.0 reduce-scatter.1
  458.1 135.5 all-gather.4
